TPU v7x, 512 devices: a whole 4x8x8 slice. The times are simulated.
512 devices in a mesh: tm: 64 (over y, x, core), head: 8 (over z).
Axes of the slice: x: 4, y: 8, z: 8, core: 2. Of those that a mesh axis runs over, the one named last changes fastest.
Arguments:
- queries: bfloat16 [24576, 5120], P('tm', 'head')
- keys: bfloat16 [24576, 5120], P('tm', 'head')
- values: bfloat16 [24576, 5120], P('tm', 'head')
- text_keys: bfloat16 [512, 5120], P('tm', 'head'), may hold values from -6 to 6
- text_values: bfloat16 [512, 5120], P('tm', 'head')
- out_weight: bfloat16 [5120, 5120], P('head', 'tm'), may hold values from -0.25 to 0.25
- windows: int32 [64], replicated, may hold values from 0 to 4, as said below
- lengths: int32 [64], replicated, may hold values from 96 to 384, as said below
Outputs:
- mixed: bfloat16 [24576, 5120], P('tm', 'head')
Inputs may be any that keep to these rules, and one draw needn't show every extreme that they name: windows reach 4 for some frame in every draw. `lengths`: some frame is full in every draw.
All inputs are finite; a program needn't handle non-finite values.
Results may differ from a plain program's by a relative error of at most 0.014.
Values may be sent and summed in bfloat16 or wider, within the bound.
No kernel may reach another device: no remote copies, remote signals or barrier semaphores. Data moves between devices by JAX's collectives and lax.ppermute only.
A program may use at most 64 MiB of HBM per device.

v0:
```python
import math
import jax
import jax.numpy as jnp
from jax import lax
from jax.sharding import PartitionSpec as P

HD = 128
WIN = 4
FRAME_AXES = ("y", "x", "c")
CHIP_AXES = ("y", "x")
GATHER_SPARE = 8


def shift_frames(value, steps):
    count = lax.axis_size(FRAME_AXES)
    return lax.ppermute(
        value, FRAME_AXES, [(source, source + steps) for source in range(count - steps)]
    )


def relay_back(value, chips_back):
    ys, xs, cs = (lax.axis_size(name) for name in FRAME_AXES)
    count = ys * xs * cs
    first, second = ([], [])
    for y in range(ys):
        for x in range(xs):
            for c in range(cs):
                source = (y * xs + x) * cs + c
                middle = (y * xs + (x - 1) % xs) * cs + c
                first.append((source, middle))
                target = source + chips_back * cs
                if target < count:
                    second.append((middle, target))
    hop = lax.ppermute(value, FRAME_AXES, first)
    return lax.ppermute(hop, FRAME_AXES, second)


def swap_cores(value):
    return lax.ppermute(value, "c", [(0, 1), (1, 0)])


def on_device(queries, keys, values, text_keys, text_values, out_weight, windows, lengths):
    rows = queries.shape[0]
    width = queries.shape[1]
    local_heads = width // HD
    groups = lax.axis_size("head")
    scale = 1.0 / math.sqrt(HD)
    position = lax.axis_index(FRAME_AXES)
    core = lax.axis_index("c")
    first_core = core == 0
    chips = lax.axis_size(CHIP_AXES)
    block = out_weight.shape[1]
    tokens = text_keys.shape[0]
    spare = jnp.zeros((width, GATHER_SPARE), out_weight.dtype)
    packed = jnp.concatenate([out_weight, text_keys.T, text_values.T, spare], axis=1)
    packed, keys, values = lax.optimization_barrier((packed, keys, values))
    packed = lax.all_gather(
        lax.all_gather(packed, "y", axis=1, tiled=True), "x", axis=1, tiled=True
    )
    own = jnp.stack([keys, values])
    back2 = shift_frames(own, 2)
    back4 = relay_back(own, 2)
    back1 = swap_cores(jnp.where(first_core, own, back2))
    back3 = swap_cores(jnp.where(first_core, back2, back4))
    kv_list = [own, back1, back2, back3, back4]
    token_ids = jnp.arange(rows, dtype=jnp.int32)
    own_window = windows[position]
    mask_list = []
    for step in range(WIN + 1):
        source = position - step
        usable = (step <= own_window) & (source >= 0)
        source_len = lengths[jnp.maximum(source, 0)]
        mask_list.append(usable & (token_ids < source_len))
    key_mask = jnp.concatenate(mask_list)
    all_keys = jnp.concatenate([p[0] for p in kv_list], axis=0)
    all_values = jnp.concatenate([p[1] for p in kv_list], axis=0)
    frame_parts = []
    for head_index in range(local_heads):
        lower = head_index * HD
        query_h = queries[:, lower : lower + HD]
        scores = (
            lax.dot_general(
                query_h,
                all_keys[:, lower : lower + HD],
                (((1,), (1,)), ((), ())),
                preferred_element_type=jnp.float32,
            )
            * scale
        )
        scores = jnp.where(key_mask[None, :], scores, -jnp.inf)
        top_f = jnp.max(scores, axis=-1, keepdims=True)
        weights = jnp.exp(scores - top_f)
        total_f = jnp.sum(weights, axis=-1, keepdims=True)
        acc_f = jnp.dot(
            weights.astype(jnp.bfloat16),
            all_values[:, lower : lower + HD],
            preferred_element_type=jnp.float32,
        )
        frame_parts.append((top_f, total_f, acc_f))
    packed, frame_parts = lax.optimization_barrier((packed, frame_parts))
    packed = packed.reshape(width, chips, -1)
    text_own = packed[:, :, block : block + 2 * tokens]
    text_pair = jnp.stack([text_own, swap_cores(text_own)])
    text_kt = text_pair[:, :, :, :tokens].transpose(1, 0, 2, 3).reshape(width, -1)
    text_vt = text_pair[:, :, :, tokens:].transpose(1, 0, 2, 3).reshape(width, -1)
    weight_own = packed[:, :, :block]
    weight_other = swap_cores(weight_own)
    weight_pair = jnp.where(
        first_core, jnp.stack([weight_own, weight_other]), jnp.stack([weight_other, weight_own])
    )
    head_outputs = []
    for head_index in range(local_heads):
        lower = head_index * HD
        query_h = queries[:, lower : lower + HD]
        top_f, total_f, acc_f = frame_parts[head_index]
        scores_t = (
            jnp.dot(query_h, text_kt[lower : lower + HD], preferred_element_type=jnp.float32)
            * scale
        )
        top_t = jnp.max(scores_t, axis=-1, keepdims=True)
        weights_t = jnp.exp(scores_t - top_t)
        total_t = jnp.sum(weights_t, axis=-1, keepdims=True)
        acc_t = lax.dot_general(
            weights_t.astype(jnp.bfloat16),
            text_vt[lower : lower + HD],
            (((1,), (1,)), ((), ())),
            preferred_element_type=jnp.float32,
        )
        top = jnp.maximum(top_f, top_t)
        keep_f = jnp.exp(top_f - top)
        keep_t = jnp.exp(top_t - top)
        attended = (acc_f * keep_f + acc_t * keep_t) / (total_f * keep_f + total_t * keep_t)
        head_outputs.append(attended.astype(jnp.bfloat16))
    attended_all = jnp.concatenate(head_outputs, axis=1)
    ys = lax.axis_size("y")
    xs = lax.axis_size("x")
    w5 = weight_pair.reshape(2, width, xs, ys, block)
    partial_out = jnp.einsum(
        "rk,ckxyn->yrcxn", attended_all, w5, preferred_element_type=jnp.float32
    )
    partial_out = partial_out.reshape(groups, rows, -1)
    mixed = lax.psum_scatter(
        partial_out.astype(jnp.bfloat16), "head", scatter_dimension=0, tiled=True
    )
    mixed = mixed.reshape(rows, 2, xs, block)
    return mixed.transpose(0, 2, 1, 3).reshape(rows, -1)


def solution(mesh):
    frames, heads = mesh.devices.shape
    cores = 2
    xs = 4 if frames % (4 * cores) == 0 else 1
    grid = mesh.devices.reshape(frames // (xs * cores), xs, cores, heads)
    fine = jax.sharding.Mesh(grid, FRAME_AXES + ("head",))
    return jax.shard_map(
        on_device,
        mesh=fine,
        in_specs=(
            P(FRAME_AXES, "head"),
            P(FRAME_AXES, "head"),
            P(FRAME_AXES, "head"),
            P(FRAME_AXES, "head"),
            P(FRAME_AXES, "head"),
            P("head", FRAME_AXES),
            P(),
            P(),
        ),
        out_specs=P(FRAME_AXES, "head"),
        check_vma=False,
    )
```

profile of v0, /device:TPU:1, one launch (start us, length us, event | category | flops | bytes accessed | tf_op | source)
XLA Modules:
  0.0 202.4 jit_solution(5313471305251070740)
XLA Ops:
  6.6 1.7 maximum_maximum_fusion
  8.4 2.3 %pad_maximum_fusion = bf16[2,384,640]{2,1,0:T(8,128)(2,1)} fusion(bf16[1,384,640]{2,1,0:T(8,128)(2,1)} %bitcast.91, bf16[1,384,640]{2,1,0:T(8,128)(2,1)} %bitcast.89), kind=kLoop, calls=%fused_computation.76 | loop fusion | flops 491520 | bytes 1966080 | tf_op jit(solution)/shard_map/stack | solution.py:60
  10.6 5.2 %collective-permute-start.2 = (bf16[2,384,640]{2,1,0:T(8,128)(2,1)}, bf16[2,384,640]{2,1,0:T(8,128)(2,1)}, u32[]{:S(2)}, u32[]{:S(2)}) collective-permute-start(bf16[2,384,640]{2,1,0:T(8,128)(2,1)} %pad_maximum_fusion), channel_id=1, source_target_pairs={{0,48},{8,56},{16,0},{24,8},{32,16},{40,24},{48,32},{56,40},{64,11... | collective-permute-start | bytes 2949128 | tf_op jit(solution)/shard_map/ppermute | solution.py:34
  15.9 1.4 collective-permute-start
  17.3 16.6 %collective-permute-done.2 = bf16[2,384,640]{2,1,0:T(8,128)(2,1)} collective-permute-done((bf16[2,384,640]{2,1,0:T(8,128)(2,1)}, bf16[2,384,640]{2,1,0:T(8,128)(2,1)}, u32[]{:S(2)}, u32[]{:S(2)}) %collective-permute-start.2) | collective-permute-done | bytes 983072 | tf_op jit(solution)/shard_map/ppermute | solution.py:34
  33.9 5.4 %collective-permute-start.3 = (bf16[2,384,640]{2,1,0:T(8,128)(2,1)}, bf16[2,384,640]{2,1,0:T(8,128)(2,1)S(1)}, u32[]{:S(2)}, u32[]{:S(2)}) collective-permute-start(bf16[2,384,640]{2,1,0:T(8,128)(2,1)} %collective-permute-done.2), channel_id=1, source_target_pairs={{48,32},{56,40},{0,48},{8,56},{16,64},{24,72},{32,80},{40,88},{112... | collective-permute-start | bytes 2949128 | tf_op jit(solution)/shard_map/ppermute | solution.py:35
  39.3 16.6 %all-gather.3.cloned.1.call-done = bf16[640,832]{0,1:T(8,128)(2,1)} async-done(((bf16[640,104]{0,1:T(8,128)(2,1)}), bf16[640,832]{0,1:T(8,128)(2,1)}) %all-gather.3.cloned.1.call-update) | async-done | bytes 1064976 | tf_op jit(solution)/shard_map/all_gather | solution.py:58
  55.9 0.4 collective-permute-done.3
  56.3 1.5 broadcast_select_fusion
  57.9 7.0 %collective-permute-start.1 = (bf16[2,384,640]{2,1,0:T(8,128)(2,1)}, bf16[2,384,640]{2,1,0:T(8,128)(2,1)}, u32[]{:S(2)}, u32[]{:S(2)}) collective-permute-start(bf16[2,384,640]{2,1,0:T(8,128)(2,1)} %get-tuple-element.71), channel_id=1, source_target_pairs={{0,8},{8,0},{1,9},{9,1},{2,10},{10,2},{3,11},{11,3},{4,12},{12,4},... | collective-permute-start | bytes 2949128 | tf_op jit(solution)/shard_map/ppermute | solution.py:39
  65.0 0.6 dynamic_slice.18
  68.8 0.7 fusion.137
  69.5 0.6 fusion.109
  70.1 0.3 dynamic-update-slice.15
  70.4 0.7 fusion.110
  71.1 0.3 dynamic-update-slice.16
  71.3 1.9 collective-permute-start.4
  73.3 0.6 fusion.111
  73.9 0.3 dynamic-update-slice.17
  74.1 0.7 fusion.112
  74.8 0.2 dynamic-update-slice.18
  75.1 0.7 fusion.113
  75.7 0.2 dynamic-update-slice.19
  76.1 1.4 fusion.82
  77.7 1.4 fusion.80
  79.3 0.7 fusion.142
  80.0 0.5 fusion.21
  80.6 0.7 fusion.141
  81.3 0.5 fusion.19
  81.8 0.7 fusion.140
  82.5 0.5 fusion.17
  83.1 0.7 fusion.139
  83.8 0.5 fusion.15
  84.3 0.7 fusion.138
  85.0 0.5 fusion.13
  85.5 0.6 fusion.22
  86.2 0.6 fusion.24
  86.8 0.6 fusion.26
  87.4 0.6 fusion.28
  88.0 0.6 fusion.30
  88.6 27.8 %all-gather.5.cloned.1.call-done = bf16[640,3328]{0,1:T(8,128)(2,1)} async-done(((bf16[640,832]{0,1:T(8,128)(2,1)}), bf16[640,3328]{0,1:T(8,128)(2,1)}) %all-gather.5.cloned.1.call-update) | async-done | bytes 4259856 | tf_op jit(solution)/shard_map/all_gather | solution.py:57
  116.4 1.2 slice_bitcast_fusion.8
  117.6 2.6 %collective-permute-start.6 = (bf16[640,32,16]{0,2,1:T(8,128)(2,1)S(1)}, bf16[640,32,16]{0,2,1:T(8,128)(2,1)S(1)}, u32[]{:S(2)}, u32[]{:S(2)}) collective-permute-start(bf16[640,32,16]{0,2,1:T(8,128)(2,1)S(1)} %get-tuple-element.59), channel_id=1, source_target_pairs={{0,8},{8,0},{1,9},{9,1},{2,10},{10,2},{3,11},{11,3},{4,12},{12,4},... | collective-permute-start | bytes 1966088 | tf_op jit(solution)/shard_map/ppermute | solution.py:39
  120.2 2.2 %slice.211 = bf16[640,32,80]{0,2,1:T(8,128)(2,1)S(1)} slice(bf16[640,32,104]{0,2,1:T(8,128)(2,1)} %bitcast.94), slice={[0:640], [0:32], [0:80]} | slice | bytes 6553600 | tf_op jit(solution)/shard_map/slice | solution.py:106
  122.4 2.1 %collective-permute-start.5 = (bf16[640,32,80]{0,2,1:T(8,128)(2,1)S(1)}, bf16[640,32,80]{0,2,1:T(8,128)(2,1)S(1)}, u32[]{:S(2)}, u32[]{:S(2)}) collective-permute-start(bf16[640,32,80]{0,2,1:T(8,128)(2,1)S(1)} %slice.211), channel_id=1, source_target_pairs={{0,8},{8,0},{1,9},{9,1},{2,10},{10,2},{3,11},{11,3},{4,12},{12,4},... | collective-permute-start | bytes 9830408 | tf_op jit(solution)/shard_map/ppermute | solution.py:39
  124.8 0.3 fusion.147
  125.1 0.3 fusion.146
  125.4 0.2 fusion.65
  125.8 0.3 fusion.145
  126.0 0.2 fusion.61
  126.2 0.3 fusion.144
  126.5 0.2 fusion.59
  126.7 0.3 fusion.143
  127.4 0.3 fusion.48
  127.7 0.4 fusion.50
  128.1 0.4 fusion.52
  128.5 0.4 fusion.54
  128.9 0.4 fusion.56
  129.3 0.8 collective-permute-done.5
  130.1 4.7 %convert_bitcast_fusion = bf16[8,384,2,4,80]{1,4,0,3,2:T(8,128)(2,1)S(1)} fusion(bf16[1,640,4,8,80]{1,4,3,2,0:T(8,128)(2,1)S(1)} %bitcast.111, bf16[1,640,4,8,80]{1,4,3,2,0:T(8,128)(2,1)S(1)} %bitcast.95, pred[]{:T(512)S(6)} %eq.3, bf16[384,640]{1,0:T(8,128)(2,1)S(1)} %fusion.56), kind=kOutput, calls=%fused_computation.8 | convolution fusion | flops 2528378880 | bytes 10977281 | tf_op jit(solution)/shard_map/rk,ckxyn->yrcxn/dot_general | solution.py:138
  134.9 2.5 %copy.9 = bf16[8,384,2,4,80]{1,4,3,2,0:T(8,128)(2,1)} copy(bf16[8,384,2,4,80]{1,4,0,3,2:T(8,128)(2,1)S(1)} %convert_bitcast_fusion) | data formatting | bytes 7864320 | tf_op jit(solution)/shard_map/convert_element_type | solution.py:143
  137.4 56.4 %reduce-scatter.2.cloned.1.call-done = bf16[1,384,640]{1,2,0:T(8,128)(2,1)} async-done(((bf16[8,384,640]{1,2,0:T(8,128)(2,1)}), bf16[1,384,640]{1,2,0:T(8,128)(2,1)}) %reduce-scatter.2.cloned.1.call-update) | async-done | bytes 491536 | tf_op jit(solution)/shard_map/reduce_scatter | solution.py:142
  193.8 1.1 copy.10
  194.9 1.0 copy.11
  (46 shorter events, 1.6 us)
Async XLA Ops:
  6.5 49.8 %copy-start.1 = (bf16[384,640]{1,0:T(8,128)(2,1)S(1)}, bf16[384,640]{1,0:T(8,128)(2,1)}, u32[]{:S(2)}) copy-start(bf16[384,640]{1,0:T(8,128)(2,1)} %param.10) | copy-start | bytes 1474564
  6.5 49.8 %copy-start = (bf16[384,640]{1,0:T(8,128)(2,1)S(1)}, bf16[384,640]{1,0:T(8,128)(2,1)}, u32[]{:S(2)}) copy-start(bf16[384,640]{1,0:T(8,128)(2,1)} %param.9) | copy-start | bytes 1474564
  6.5 49.3 %all-gather.3.cloned.1.call-start = ((), (), s32[]{:S(2)}) async-start(), calls=%async_computation.1 | async-start | bytes 1198080 | tf_op jit(solution)/shard_map/all_gather | solution.py:58
  10.6 23.3 %collective-permute-start.2 = (bf16[2,384,640]{2,1,0:T(8,128)(2,1)}, bf16[2,384,640]{2,1,0:T(8,128)(2,1)}, u32[]{:S(2)}, u32[]{:S(2)}) collective-permute-start(bf16[2,384,640]{2,1,0:T(8,128)(2,1)} %pad_maximum_fusion), channel_id=1, source_target_pairs={{0,48},{8,56},{16,0},{24,8},{32,16},{40,24},{48,32},{56,40},{64,11... | collective-permute-start | bytes 2949128 | tf_op jit(solution)/shard_map/ppermute | solution.py:34
  15.9 100.5 %all-gather.5.cloned.1.call-start = ((), (), s32[]{:S(2)}) async-start(), calls=%async_computation.2 | async-start | bytes 5324800 | tf_op jit(solution)/shard_map/all_gather | solution.py:57
  15.9 40.0 %collective-permute-start = (bf16[2,384,640]{2,1,0:T(8,128)(2,1)}, bf16[2,384,640]{2,1,0:T(8,128)(2,1)S(1)}, u32[]{:S(2)}, u32[]{:S(2)}) collective-permute-start(bf16[2,384,640]{2,1,0:T(8,128)(2,1)} %pad_maximum_fusion), channel_id=1, source_target_pairs={{0,16},{8,24},{16,32},{24,40},{32,48},{40,56},{48,64},{56,72},{64,... | collective-permute-start | bytes 2949128 | tf_op jit(solution)/shard_map/ppermute | solution.py:16
  33.9 22.4 %collective-permute-start.3 = (bf16[2,384,640]{2,1,0:T(8,128)(2,1)}, bf16[2,384,640]{2,1,0:T(8,128)(2,1)S(1)}, u32[]{:S(2)}, u32[]{:S(2)}) collective-permute-start(bf16[2,384,640]{2,1,0:T(8,128)(2,1)} %collective-permute-done.2), channel_id=1, source_target_pairs={{48,32},{56,40},{0,48},{8,56},{16,64},{24,72},{32,80},{40,88},{112... | collective-permute-start | bytes 2949128 | tf_op jit(solution)/shard_map/ppermute | solution.py:35
  55.8 9.1 %copy-start.4 = (s32[64]{0:T(128)S(1)}, s32[64]{0:T(128)}, u32[]{:S(2)}) copy-start(s32[64]{0:T(128)} %param.14) | copy-start | bytes 772
  55.8 13.0 %copy-start.3 = (s32[64]{0:T(128)S(1)}, s32[64]{0:T(128)}, u32[]{:S(2)}) copy-start(s32[64]{0:T(128)} %param.15) | copy-start | bytes 772
  55.9 137.9 %reduce-scatter.2.cloned.1.call-start = ((), (), s32[]{:S(2)}) async-start(), calls=%async_computation.3 | async-start | bytes 4423680 | tf_op jit(solution)/shard_map/reduce_scatter | solution.py:142
  57.9 18.2 %collective-permute-start.1 = (bf16[2,384,640]{2,1,0:T(8,128)(2,1)}, bf16[2,384,640]{2,1,0:T(8,128)(2,1)}, u32[]{:S(2)}, u32[]{:S(2)}) collective-permute-start(bf16[2,384,640]{2,1,0:T(8,128)(2,1)} %get-tuple-element.71), channel_id=1, source_target_pairs={{0,8},{8,0},{1,9},{9,1},{2,10},{10,2},{3,11},{11,3},{4,12},{12,4},... | collective-permute-start | bytes 2949128 | tf_op jit(solution)/shard_map/ppermute | solution.py:39
  71.3 6.4 %collective-permute-start.4 = (bf16[2,384,640]{2,1,0:T(8,128)(2,1)}, bf16[2,384,640]{2,1,0:T(8,128)(2,1)}, u32[]{:S(2)}, u32[]{:S(2)}) collective-permute-start(bf16[2,384,640]{2,1,0:T(8,128)(2,1)} %get-tuple-element.70), channel_id=1, source_target_pairs={{0,8},{8,0},{1,9},{9,1},{2,10},{10,2},{3,11},{11,3},{4,12},{12,4},... | collective-permute-start | bytes 2949128 | tf_op jit(solution)/shard_map/ppermute | solution.py:39
  77.5 1.8 copy-start.2
  117.6 6.9 %collective-permute-start.6 = (bf16[640,32,16]{0,2,1:T(8,128)(2,1)S(1)}, bf16[640,32,16]{0,2,1:T(8,128)(2,1)S(1)}, u32[]{:S(2)}, u32[]{:S(2)}) collective-permute-start(bf16[640,32,16]{0,2,1:T(8,128)(2,1)S(1)} %get-tuple-element.59), channel_id=1, source_target_pairs={{0,8},{8,0},{1,9},{9,1},{2,10},{10,2},{3,11},{11,3},{4,12},{12,4},... | collective-permute-start | bytes 1966088 | tf_op jit(solution)/shard_map/ppermute | solution.py:39
  122.4 7.7 %collective-permute-start.5 = (bf16[640,32,80]{0,2,1:T(8,128)(2,1)S(1)}, bf16[640,32,80]{0,2,1:T(8,128)(2,1)S(1)}, u32[]{:S(2)}, u32[]{:S(2)}) collective-permute-start(bf16[640,32,80]{0,2,1:T(8,128)(2,1)S(1)} %slice.211), channel_id=1, source_target_pairs={{0,8},{8,0},{1,9},{9,1},{2,10},{10,2},{3,11},{11,3},{4,12},{12,4},... | collective-permute-start | bytes 9830408 | tf_op jit(solution)/shard_map/ppermute | solution.py:39
Sparse Core Ops, SparseCore 0:
  16.0 39.8 all-gather.2
  57.9 58.4 all-gather.4
  137.5 56.2 reduce-scatter.1
where the time goes:
time: 203 us; the launch traced here: 202 us
  waiting for transfers between devices  119 us (59%)
  starting transfers between devices  25.6 us (13%)
  between operations  16.7 us (8%)
  matrix products  14.7 us (7%)
  local copies, waits for them, and re-layouts  14.2 us (7%)
  other arithmetic  12.5 us (6%)
    reduce_scatter x1, waiting for transfers between devices, on_device(): lax.psum_scatter(partial_out.astype(jnp.bfloat16), 'head', scatter_dimens...  56.4 us
    all_gather x1, waiting for transfers between devices, on_device(): lax.all_gather(lax.all_gather(packed, 'y', axis=1, tiled=True), 'x', axis...  27.8 us
    ppermute x1, waiting for transfers between devices, relay_back(): hop = lax.ppermute(value, FRAME_AXES, first)  16.6 us
    all_gather x1, waiting for transfers between devices, on_device(): lax.all_gather(packed, 'y', axis=1, tiled=True)  16.6 us
    ppermute x4, starting transfers between devices, swap_cores(): return lax.ppermute(value, 'c', [(0, 1), (1, 0)])  13.6 us
    ppermute x1, starting transfers between devices, relay_back(): return lax.ppermute(hop, FRAME_AXES, second)  5.36 us
    ppermute x1, starting transfers between devices, relay_back(): hop = lax.ppermute(value, FRAME_AXES, first)  5.21 us
    dot_general x1, matrix products, on_device(): jnp.einsum('rk,ckxyn->yrcxn', attended_all, w5, preferred_element_type=jn...  4.72 us
  transfers between devices with their start and end apart: 10, of which 6 were waited for; matrix products, arithmetic and copies ran while one was open for 13% of the time, Pallas kernels for 0%

commit v1 on v0

--- a/solution.py
+++ b/solution.py
@@ -54,8 +54,14 @@
     spare = jnp.zeros((width, GATHER_SPARE), out_weight.dtype)
     packed = jnp.concatenate([out_weight, text_keys.T, text_values.T, spare], axis=1)
     packed, keys, values = lax.optimization_barrier((packed, keys, values))
-    packed = lax.all_gather(
-        lax.all_gather(packed, "y", axis=1, tiled=True), "x", axis=1, tiled=True
+    packed = jnp.concatenate(
+        lax.all_to_all(
+            jnp.stack([lax.all_gather(packed, "y", axis=1, tiled=True)] * lax.axis_size("x")),
+            "x",
+            0,
+            0,
+        ),
+        axis=1,
     )
     own = jnp.stack([keys, values])
     back2 = shift_frames(own, 2)

time: 203 us -> 236 us (1.16)
  waiting for transfers between devices: 119 us -> 130 us
  starting transfers between devices: 25.6 us -> 35.6 us
  local copies, waits for them, and re-layouts: 14.2 us -> 22.6 us
    all_to_all x0 -> x1, waiting for transfers between devices: none -> 28.1 us  [on_device(): lax.all_to_all(jnp.stack([lax.all_gather(packed, 'y', axis=1, tiled=True)...]
    all_gather x1 -> x0, waiting for transfers between devices: 27.8 us -> none  [on_device(): lax.all_gather(lax.all_gather(packed, 'y', axis=1, tiled=True), 'x', axis...]
    ppermute x1, waiting for transfers between devices: 0.39 us -> 17 us  [relay_back(): return lax.ppermute(hop, FRAME_AXES, second)]
    all_gather x1, waiting for transfers between devices: 16.6 us -> 3.48 us  [on_device(): lax.all_gather(packed, 'y', axis=1, tiled=True)]
    reduce_scatter x1, waiting for transfers between devices: 56.4 us -> 64.2 us  [on_device(): lax.psum_scatter(partial_out.astype(jnp.bfloat16), 'head', scatter_dimens...]
    all_to_all x0 -> x1, starting transfers between devices: none -> 5.41 us  [on_device(): lax.all_to_all(jnp.stack([lax.all_gather(packed, 'y', axis=1, tiled=True)...]
    ppermute x4, starting transfers between devices: 13.6 us -> 18.1 us  [swap_cores(): return lax.ppermute(value, 'c', [(0, 1), (1, 0)])]
    unnamed x18 -> x22, local copies, waits for them, and re-layouts: 4.13 us -> 7.98 us
  transfers between devices with their start and end apart: 10 -> 10, of which waited for: 6 -> 6; matrix products, arithmetic and copies ran while one was open for 13% -> 16% of each run, Pallas kernels for 0% -> 0%
where the time goes in v1:
time: 236 us; the launch traced here: 235 us
  waiting for transfers between devices  130 us (55%)
  starting transfers between devices  35.6 us (15%)
  local copies, waits for them, and re-layouts  22.6 us (10%)
  between operations  17.2 us (7%)
  matrix products  16.4 us (7%)
  other arithmetic  13.3 us (6%)
    reduce_scatter x1, waiting for transfers between devices, on_device(): lax.psum_scatter(partial_out.astype(jnp.bfloat16), 'head', scatter_dimens...  64.2 us
    all_to_all x1, waiting for transfers between devices, on_device(): lax.all_to_all(jnp.stack([lax.all_gather(packed, 'y', axis=1, tiled=True)...  28.1 us
    ppermute x4, starting transfers between devices, swap_cores(): return lax.ppermute(value, 'c', [(0, 1), (1, 0)])  18.1 us
    ppermute x1, waiting for transfers between devices, relay_back(): return lax.ppermute(hop, FRAME_AXES, second)  17 us
    ppermute x1, waiting for transfers between devices, relay_back(): hop = lax.ppermute(value, FRAME_AXES, first)  16.7 us
    unnamed x22, local copies, waits for them, and re-layouts  7.98 us
    all_to_all x1, starting transfers between devices, on_device(): lax.all_to_all(jnp.stack([lax.all_gather(packed, 'y', axis=1, tiled=True)...  5.41 us
    ppermute x1, starting transfers between devices, relay_back(): return lax.ppermute(hop, FRAME_AXES, second)  5.36 us
  transfers between devices with their start and end apart: 10, of which 6 were waited for; matrix products, arithmetic and copies ran while one was open for 16% of the time, Pallas kernels for 0%

profile of v1, /device:TPU:1, one launch (start us, length us, event | category | flops | bytes accessed | tf_op | source)
XLA Modules:
  0.0 235.4 jit_solution(374098044255019366)
XLA Ops:
  6.6 1.7 maximum_maximum_fusion
  8.3 2.2 pad_maximum_fusion
  10.5 5.3 %collective-permute-start.2 = (bf16[2,384,640]{2,1,0:T(8,128)(2,1)}, bf16[2,384,640]{2,1,0:T(8,128)(2,1)}, u32[]{:S(2)}, u32[]{:S(2)}) collective-permute-start(bf16[2,384,640]{2,1,0:T(8,128)(2,1)} %pad_maximum_fusion), channel_id=1, source_target_pairs={{0,48},{8,56},{16,0},{24,8},{32,16},{40,24},{48,32},{56,40},{64,11... | collective-permute-start | bytes 2949128 | tf_op jit(solution)/shard_map/ppermute | solution.py:34
  15.9 1.4 collective-permute-start
  17.3 16.7 %collective-permute-done.2 = bf16[2,384,640]{2,1,0:T(8,128)(2,1)} collective-permute-done((bf16[2,384,640]{2,1,0:T(8,128)(2,1)}, bf16[2,384,640]{2,1,0:T(8,128)(2,1)}, u32[]{:S(2)}, u32[]{:S(2)}) %collective-permute-start.2) | collective-permute-done | bytes 983072 | tf_op jit(solution)/shard_map/ppermute | solution.py:34
  33.9 5.4 %collective-permute-start.3 = (bf16[2,384,640]{2,1,0:T(8,128)(2,1)}, bf16[2,384,640]{2,1,0:T(8,128)(2,1)S(1)}, u32[]{:S(2)}, u32[]{:S(2)}) collective-permute-start(bf16[2,384,640]{2,1,0:T(8,128)(2,1)} %collective-permute-done.2), channel_id=1, source_target_pairs={{48,32},{56,40},{0,48},{8,56},{16,64},{24,72},{32,80},{40,88},{112... | collective-permute-start | bytes 2949128 | tf_op jit(solution)/shard_map/ppermute | solution.py:35
  39.4 17.0 %collective-permute-done.3 = bf16[2,384,640]{2,1,0:T(8,128)(2,1)S(1)} collective-permute-done((bf16[2,384,640]{2,1,0:T(8,128)(2,1)}, bf16[2,384,640]{2,1,0:T(8,128)(2,1)S(1)}, u32[]{:S(2)}, u32[]{:S(2)}) %collective-permute-start.3) | collective-permute-done | bytes 983072 | tf_op jit(solution)/shard_map/ppermute | solution.py:35
  56.4 2.6 %broadcast_select_fusion = (bf16[2,384,640]{2,1,0:T(8,128)(2,1)}, bf16[2,384,640]{2,1,0:T(8,128)(2,1)}) fusion(bf16[2,384,640]{2,1,0:T(8,128)(2,1)S(1)} %collective-permute-done, bf16[2,384,640]{2,1,0:T(8,128)(2,1)S(1)} %collective-permute-done.3, pred[]{:T(512)S(6)} %eq.3, bf16[1,384,640]{2,1,0:T(8,128)(2,1)} %bitcast.95, bf16[1,384,640]{2,1,0:T(8,128)(2,1)} %bitcast.93), kind=kLoop, calls=%fused_computation.77 | loop fusion | flops 1474560 | bytes 4915201 | tf_op jit(solution)/shard_map/jit(_where)/select_n | solution.py:70
  59.0 7.0 %collective-permute-start.1 = (bf16[2,384,640]{2,1,0:T(8,128)(2,1)}, bf16[2,384,640]{2,1,0:T(8,128)(2,1)}, u32[]{:S(2)}, u32[]{:S(2)}) collective-permute-start(bf16[2,384,640]{2,1,0:T(8,128)(2,1)} %get-tuple-element.71), channel_id=1, source_target_pairs={{0,8},{8,0},{1,9},{9,1},{2,10},{10,2},{3,11},{11,3},{4,12},{12,4},... | collective-permute-start | bytes 2949128 | tf_op jit(solution)/shard_map/ppermute | solution.py:39
  66.1 0.7 dynamic_slice.18
  70.3 0.7 fusion.137
  70.9 0.6 fusion.109
  71.6 0.3 dynamic-update-slice.15
  71.8 0.6 fusion.110
  72.5 0.3 dynamic-update-slice.16
  72.7 1.9 collective-permute-start.4
  74.6 0.6 fusion.111
  75.4 0.6 fusion.112
  76.3 0.7 fusion.113
  77.3 1.1 constant_dynamic-update-slice_fusion
  78.3 3.5 %all-gather.2.cloned.1.call-done = bf16[640,832]{0,1:T(8,128)(2,1)} async-done(((bf16[640,104]{0,1:T(8,128)(2,1)}), bf16[640,832]{0,1:T(8,128)(2,1)}) %all-gather.2.cloned.1.call-update) | async-done | bytes 1064976 | tf_op jit(solution)/shard_map/all_gather | solution.py:59
  81.8 3.5 %stack.39 = bf16[4,640,832]{1,2,0:T(8,128)(2,1)} broadcast(bf16[640,832]{0,1:T(8,128)(2,1)} %all-gather.2.cloned.1.call-done), dimensions={1,2} | broadcast | bytes 5324800 | tf_op jit(solution)/shard_map/stack | solution.py:59
  85.3 5.4 %all-to-all-start = ((bf16[4,640,832]{1,2,0:T(8,128)(2,1)}), bf16[4,640,832]{1,2,0:T(8,128)(2,1)}, u32[]{:S(2)}, u32[]{:S(2)}) async-start(bf16[4,640,832]{1,2,0:T(8,128)(2,1)} %stack.39), calls=%async_computation | async-start | bytes 8519680 | tf_op jit(solution)/shard_map/all_to_all | solution.py:58
  90.8 2.2 fusion.82
  93.0 1.0 fusion.81
  94.0 2.2 fusion.80
  96.2 1.1 fusion.79
  97.3 2.4 %fusion.142 = (f32[384]{0:T(512)S(1)}, f32[1920,384]{1,0:T(8,128)S(1)}) fusion(bf16[384,640]{1,0:T(8,128)(2,1)S(1)} %copy-done.4, bf16[1920,640]{1,0:T(8,128)(2,1)} %get-tuple-element.63, pred[1920]{0:T(1024)(128)(4,1)S(1)} %dynamic-update-slice.19), kind=kOutput, calls=%fused_computation.197 | convolution fusion | flops 190955136 | bytes 3542528 | tf_op jit(solution)/shard_map/dot_general | solution.py:88
  99.7 0.7 fusion.141
  100.4 0.5 fusion.21
  101.0 0.5 fusion.19
  101.5 0.7 fusion.140
  102.2 0.5 fusion.17
  102.7 0.7 fusion.139
  103.4 0.5 fusion.15
  104.0 0.7 fusion.138
  104.7 0.5 fusion.13
  105.2 0.4 copy-done.2
  105.6 0.6 fusion.22
  106.3 0.6 fusion.24
  106.9 0.6 fusion.26
  107.5 0.6 fusion.28
  108.1 0.6 fusion.30
  108.7 28.1 %all-to-all-done = bf16[4,640,832]{1,2,0:T(8,128)(2,1)} async-done(((bf16[4,640,832]{1,2,0:T(8,128)(2,1)}), bf16[4,640,832]{1,2,0:T(8,128)(2,1)}, u32[]{:S(2)}, u32[]{:S(2)}) %all-to-all-start) | async-done | bytes 4259872 | tf_op jit(solution)/shard_map/all_to_all | solution.py:58
  136.8 1.2 slice_bitcast_fusion.8
  138.0 7.0 %collective-permute-start.6 = (bf16[640,32,16]{0,2,1:T(8,128)(2,1)S(1)}, bf16[640,32,16]{0,2,1:T(8,128)(2,1)S(1)}, u32[]{:S(2)}, u32[]{:S(2)}) collective-permute-start(bf16[640,32,16]{0,2,1:T(8,128)(2,1)S(1)} %get-tuple-element.59), channel_id=1, source_target_pairs={{0,8},{8,0},{1,9},{9,1},{2,10},{10,2},{3,11},{11,3},{4,12},{12,4},... | collective-permute-start | bytes 1966088 | tf_op jit(solution)/shard_map/ppermute | solution.py:39
  145.0 2.2 slice.211
  147.2 2.1 collective-permute-start.5
  149.7 0.3 fusion.147
  150.0 0.3 fusion.146
  150.6 0.3 fusion.145
  151.1 0.3 fusion.144
  151.6 0.3 fusion.143
  152.2 0.3 fusion.48
  152.6 0.4 fusion.50
  153.0 0.4 fusion.52
  153.4 0.4 fusion.54
  153.8 0.4 fusion.56
  154.2 0.8 collective-permute-done.5
  155.0 4.8 %convert_bitcast_fusion = bf16[8,384,2,4,80]{1,4,0,3,2:T(8,128)(2,1)S(1)} fusion(bf16[1,640,4,8,80]{1,4,3,2,0:T(8,128)(2,1)S(1)} %bitcast.112, bf16[1,640,4,8,80]{1,4,3,2,0:T(8,128)(2,1)S(1)} %bitcast.96, pred[]{:T(512)S(6)} %eq.3, bf16[384,640]{1,0:T(8,128)(2,1)S(1)} %fusion.56), kind=kOutput, calls=%fused_computation.8 | convolution fusion | flops 2528378880 | bytes 10977281 | tf_op jit(solution)/shard_map/rk,ckxyn->yrcxn/dot_general | solution.py:144
  159.8 2.5 %copy.9 = bf16[8,384,2,4,80]{1,4,3,2,0:T(8,128)(2,1)} copy(bf16[8,384,2,4,80]{1,4,0,3,2:T(8,128)(2,1)S(1)} %convert_bitcast_fusion) | data formatting | bytes 7864320 | tf_op jit(solution)/shard_map/convert_element_type | solution.py:149
  162.3 64.2 %reduce-scatter.2.cloned.1.call-done = bf16[1,384,640]{1,2,0:T(8,128)(2,1)} async-done(((bf16[8,384,640]{1,2,0:T(8,128)(2,1)}), bf16[1,384,640]{1,2,0:T(8,128)(2,1)}) %reduce-scatter.2.cloned.1.call-update) | async-done | bytes 491536 | tf_op jit(solution)/shard_map/reduce_scatter | solution.py:148
  226.5 1.1 copy.10
  227.6 1.0 copy.11
  (50 shorter events, 2.3 us)
Async XLA Ops:
  6.5 75.3 %all-gather.2.cloned.1.call-start = ((), (), s32[]{:S(2)}) async-start(), calls=%async_computation.2 | async-start | bytes 1198080 | tf_op jit(solution)/shard_map/all_gather | solution.py:59
  10.5 55.6 %copy-start.6 = (s32[64]{0:T(128)S(1)}, s32[64]{0:T(128)}, u32[]{:S(2)}) copy-start(s32[64]{0:T(128)} %param.14) | copy-start | bytes 772
  10.5 59.7 %copy-start.5 = (s32[64]{0:T(128)S(1)}, s32[64]{0:T(128)}, u32[]{:S(2)}) copy-start(s32[64]{0:T(128)} %param.15) | copy-start | bytes 772
  10.5 66.7 %copy-start = (bf16[384,640]{1,0:T(8,128)(2,1)S(1)}, bf16[384,640]{1,0:T(8,128)(2,1)}, u32[]{:S(2)}) copy-start(bf16[384,640]{1,0:T(8,128)(2,1)} %param.9) | copy-start | bytes 1474564
  10.5 66.7 %copy-start.1 = (bf16[384,640]{1,0:T(8,128)(2,1)S(1)}, bf16[384,640]{1,0:T(8,128)(2,1)}, u32[]{:S(2)}) copy-start(bf16[384,640]{1,0:T(8,128)(2,1)} %param.10) | copy-start | bytes 1474564
  10.5 23.4 %collective-permute-start.2 = (bf16[2,384,640]{2,1,0:T(8,128)(2,1)}, bf16[2,384,640]{2,1,0:T(8,128)(2,1)}, u32[]{:S(2)}, u32[]{:S(2)}) collective-permute-start(bf16[2,384,640]{2,1,0:T(8,128)(2,1)} %pad_maximum_fusion), channel_id=1, source_target_pairs={{0,48},{8,56},{16,0},{24,8},{32,16},{40,24},{48,32},{56,40},{64,11... | collective-permute-start | bytes 2949128 | tf_op jit(solution)/shard_map/ppermute | solution.py:34
  15.9 23.4 %collective-permute-start = (bf16[2,384,640]{2,1,0:T(8,128)(2,1)}, bf16[2,384,640]{2,1,0:T(8,128)(2,1)S(1)}, u32[]{:S(2)}, u32[]{:S(2)}) collective-permute-start(bf16[2,384,640]{2,1,0:T(8,128)(2,1)} %pad_maximum_fusion), channel_id=1, source_target_pairs={{0,16},{8,24},{16,32},{24,40},{32,48},{40,56},{48,64},{56,72},{64,... | collective-permute-start | bytes 2949128 | tf_op jit(solution)/shard_map/ppermute | solution.py:16
  33.9 22.4 %collective-permute-start.3 = (bf16[2,384,640]{2,1,0:T(8,128)(2,1)}, bf16[2,384,640]{2,1,0:T(8,128)(2,1)S(1)}, u32[]{:S(2)}, u32[]{:S(2)}) collective-permute-start(bf16[2,384,640]{2,1,0:T(8,128)(2,1)} %collective-permute-done.2), channel_id=1, source_target_pairs={{48,32},{56,40},{0,48},{8,56},{16,64},{24,72},{32,80},{40,88},{112... | collective-permute-start | bytes 2949128 | tf_op jit(solution)/shard_map/ppermute | solution.py:35
  59.0 31.7 %collective-permute-start.1 = (bf16[2,384,640]{2,1,0:T(8,128)(2,1)}, bf16[2,384,640]{2,1,0:T(8,128)(2,1)}, u32[]{:S(2)}, u32[]{:S(2)}) collective-permute-start(bf16[2,384,640]{2,1,0:T(8,128)(2,1)} %get-tuple-element.71), channel_id=1, source_target_pairs={{0,8},{8,0},{1,9},{9,1},{2,10},{10,2},{3,11},{11,3},{4,12},{12,4},... | collective-permute-start | bytes 2949128 | tf_op jit(solution)/shard_map/ppermute | solution.py:39
  72.7 21.3 %collective-permute-start.4 = (bf16[2,384,640]{2,1,0:T(8,128)(2,1)}, bf16[2,384,640]{2,1,0:T(8,128)(2,1)}, u32[]{:S(2)}, u32[]{:S(2)}) collective-permute-start(bf16[2,384,640]{2,1,0:T(8,128)(2,1)} %get-tuple-element.70), channel_id=1, source_target_pairs={{0,8},{8,0},{1,9},{9,1},{2,10},{10,2},{3,11},{11,3},{4,12},{12,4},... | collective-permute-start | bytes 2949128 | tf_op jit(solution)/shard_map/ppermute | solution.py:39
  85.3 51.5 %all-to-all-start = ((bf16[4,640,832]{1,2,0:T(8,128)(2,1)}), bf16[4,640,832]{1,2,0:T(8,128)(2,1)}, u32[]{:S(2)}, u32[]{:S(2)}) async-start(bf16[4,640,832]{1,2,0:T(8,128)(2,1)} %stack.39), calls=%async_computation | async-start | bytes 8519680 | tf_op jit(solution)/shard_map/all_to_all | solution.py:58
  90.7 135.7 %reduce-scatter.2.cloned.1.call-start = ((), (), s32[]{:S(2)}) async-start(), calls=%async_computation.3 | async-start | bytes 4423680 | tf_op jit(solution)/shard_map/reduce_scatter | solution.py:148
  93.0 4.3 %copy-start.4 = (bf16[384,640]{1,0:T(8,128)(2,1)S(1)}, bf16[384,640]{1,0:T(8,128)(2,1)}, u32[]{:S(2)}) copy-start(bf16[384,640]{1,0:T(8,128)(2,1)} %param.8) | copy-start | bytes 1474564
  97.3 2.4 %copy-start.3 = (bf16[1920,640]{1,0:T(8,128)(2,1)S(1)}, bf16[1920,640]{1,0:T(8,128)(2,1)}, u32[]{:S(2)}) copy-start(bf16[1920,640]{1,0:T(8,128)(2,1)} %get-tuple-element.63) | copy-start | bytes 7372804
  103.9 1.7 copy-start.2
  138.0 11.4 %collective-permute-start.6 = (bf16[640,32,16]{0,2,1:T(8,128)(2,1)S(1)}, bf16[640,32,16]{0,2,1:T(8,128)(2,1)S(1)}, u32[]{:S(2)}, u32[]{:S(2)}) collective-permute-start(bf16[640,32,16]{0,2,1:T(8,128)(2,1)S(1)} %get-tuple-element.59), channel_id=1, source_target_pairs={{0,8},{8,0},{1,9},{9,1},{2,10},{10,2},{3,11},{11,3},{4,12},{12,4},... | collective-permute-start | bytes 1966088 | tf_op jit(solution)/shard_map/ppermute | solution.py:39
  147.2 7.7 %collective-permute-start.5 = (bf16[640,32,80]{0,2,1:T(8,128)(2,1)S(1)}, bf16[640,32,80]{0,2,1:T(8,128)(2,1)S(1)}, u32[]{:S(2)}, u32[]{:S(2)}) collective-permute-start(bf16[640,32,80]{0,2,1:T(8,128)(2,1)S(1)} %slice.211), channel_id=1, source_target_pairs={{0,8},{8,0},{1,9},{9,1},{2,10},{10,2},{3,11},{11,3},{4,12},{12,4},... | collective-permute-start | bytes 9830408 | tf_op jit(solution)/shard_map/ppermute | solution.py:39
Sparse Core Ops, SparseCore 0:
  39.5 42.3 all-gather.1
  162.4 64.0 reduce-scatter.1
